TPU v7x, 512 devices: a whole 4x8x8 slice. The times are simulated.
512 devices in a mesh: row: 4 (over y_hi), col: 16 (over y_lo, x, core), depth: 8 (over z).
Axes of the slice: x: 4, y: 8 (y_hi: 4, y_lo: 2; y = y_hi * 2 + y_lo), z: 8, core: 2. Of those that a mesh axis runs over, the one named last changes fastest.
Arguments:
- block_values: bfloat16 [32, 16, 16, 128, 128], P(('row', 'depth'), 'col'), may hold values from 0.0049743652 to 0.5
- block_cols: int32 [32, 16, 16], P(('row', 'depth'), 'col'), may hold values from 0 to 511, as said below
- live_count: int32 [32, 16], P(('row', 'depth'), 'col'), may hold values from 8 to 16, as said below
- out_pattern: int32 [4, 16, 32, 2], P('row', 'col'), may hold values from 0 to 511, as said below
Outputs:
- squared_log: bfloat16 [4, 16, 32, 128, 128], P('row', 'col', 'depth')
Inputs may be any that keep to these rules, and one draw needn't show every extreme that they name: Block row i's blocks are its first live_count slots; in every draw some block row is full. `block_cols`: the slots of one block row name distinct block columns. Call (k // 16) % 8 the depth part of a block index k and k // 32 its column group. Among the live slots of one block row at most 2 name a column in any one depth part and at most 2 in any one column group; both bounds are reached in every draw. The 32 entries of out_pattern[r, c] are distinct pairs (i, j) with i // 128 == r and j // 32 == c.
All inputs are finite; a program needn't handle non-finite values.
Results may differ from a plain program's by a relative error of at most 0.001.
Values may be sent and summed in bfloat16 or wider, within the bound.
No kernel may reach another device: no remote copies, remote signals or barrier semaphores. Data moves between devices by JAX's collectives and lax.ppermute only.
A program may use at most 128 MiB of HBM per device.

v0:
```python
import math
import jax
import jax.numpy as jnp
from jax import lax
from jax.sharding import PartitionSpec as P


def pack_slots(values, col_ids, targets, is_live, part_count, capacity):
    row_count = col_ids.shape[0]
    block_size = values.shape[-1]
    chosen = (
        targets[:, :, None] == jnp.arange(part_count, dtype=jnp.int32)[None, None, :]
    ) & is_live[:, :, None]
    running = jnp.cumsum(chosen.astype(jnp.int32), axis=1) - 1
    order_in = jnp.sum(jnp.where(chosen, running, 0), axis=2)
    row_ids = jnp.arange(row_count, dtype=jnp.int32)[:, None]
    total = part_count * row_count * capacity
    position = (targets * row_count + row_ids) * capacity + order_in
    position = jnp.where(is_live, position, total).reshape(-1)
    packed = jnp.zeros((total, block_size, block_size), values.dtype)
    packed = packed.at[position].set(values.reshape(-1, block_size, block_size), mode="drop")
    packed_cols = (
        jnp.full((total,), -1, jnp.int32).at[position].set(col_ids.reshape(-1), mode="drop")
    )
    return (
        packed.reshape(part_count, row_count, capacity, block_size, block_size),
        packed_cols.reshape(part_count, row_count, capacity),
    )


def gather_by_exchange(x, axis, size):
    copies = jnp.broadcast_to(x[None], (size,) + x.shape)
    return lax.all_to_all(copies, axis, split_axis=0, concat_axis=0, tiled=True)


def body(block_values, block_cols, live_count, out_pattern):
    depths = lax.axis_size("depth")
    columns = lax.axis_size("col")
    row_groups = lax.axis_size("row")
    row_index = lax.axis_index("row")
    rows_dev = block_values.shape[1]
    slot_count = block_values.shape[2]
    block_size = block_values.shape[3]
    group_rows = columns * rows_dev
    group_count = row_groups * depths
    total_rows = group_count * group_rows
    col_block = total_rows // columns
    pair_size = group_count // columns
    cap_left = slot_count // depths
    cap_right = pair_size * (slot_count // group_count) + min(pair_size, slot_count % group_count)
    values = block_values.reshape(rows_dev, slot_count, block_size, block_size)
    col_ids = block_cols.reshape(rows_dev, slot_count)
    counts = live_count.reshape(rows_dev)
    is_live = jnp.arange(slot_count, dtype=jnp.int32)[None, :] < counts[:, None]
    left_vals, left_cols = pack_slots(
        values, col_ids, col_ids // group_rows % depths, is_live, depths, cap_left
    )
    left_vals, left_cols = (
        lax.all_to_all(left_vals, "depth", split_axis=0, concat_axis=0, tiled=True),
        lax.all_to_all(left_cols, "depth", split_axis=0, concat_axis=0, tiled=True),
    )
    left_vals, left_cols = (
        lax.all_gather(left_vals[None], "col", axis=0, tiled=True),
        gather_by_exchange(left_cols, "col", columns),
    )
    left_shape = left_cols.shape
    source_col = lax.broadcasted_iota(jnp.int32, left_shape, 0)
    source_depth = lax.broadcasted_iota(jnp.int32, left_shape, 1)
    source_row = lax.broadcasted_iota(jnp.int32, left_shape, 2)
    left_rows = (
        (row_index * depths + source_depth) * group_rows + source_col * rows_dev + source_row
    ).reshape(-1)
    left_flat = left_vals.reshape(-1, block_size, block_size)
    left_ids = left_cols.reshape(-1)
    right_vals, right_cols = pack_slots(
        values, col_ids, col_ids // col_block, is_live, columns, cap_right
    )
    right_vals, right_cols = (
        lax.all_to_all(right_vals, "col", split_axis=0, concat_axis=0, tiled=True),
        lax.all_to_all(right_cols, "col", split_axis=0, concat_axis=0, tiled=True),
    )
    right_vals, right_cols = (
        lax.all_gather(right_vals[None], "row", axis=0, tiled=True),
        gather_by_exchange(right_cols, "row", row_groups),
    )
    right_flat = right_vals.reshape(-1, cap_right, block_size, block_size)
    right_ids = right_cols.reshape(-1, cap_right)
    pattern_rows = out_pattern[0, 0, :, 0]
    pattern_cols = out_pattern[0, 0, :, 1]
    local_row = pattern_rows - row_index * (depths * group_rows)
    left_pos = local_row % group_rows * depths + local_row // group_rows
    left_sel = left_pos[:, None] * cap_left + jnp.arange(cap_left, dtype=jnp.int32)[None, :]
    left_flat = left_vals.reshape(-1, block_size, block_size)
    left_ids = left_cols.reshape(-1)
    left_pick = jnp.take(left_flat, left_sel.reshape(-1), axis=0)
    inner = jnp.take(left_ids, left_sel, axis=0)
    safe_inner = jnp.maximum(inner, 0)
    right_row = safe_inner // (depths * group_rows) * columns + safe_inner % group_rows
    right_ids = right_cols.reshape(-1, cap_right)
    right_flat = right_vals.reshape(-1, block_size, block_size)
    right_here = jnp.take(right_ids, right_row, axis=0)
    matched = (right_here == pattern_cols[:, None, None]) & (inner >= 0)[:, :, None]
    slot = jnp.sum(
        jnp.where(matched, jnp.arange(cap_right, dtype=jnp.int32)[None, None, :], 0), axis=2
    )
    found = jnp.any(matched, axis=2)
    right_pick = jnp.take(right_flat, (right_row * cap_right + slot).reshape(-1), axis=0)
    right_pick = jnp.where(found.reshape(-1)[:, None, None], right_pick, jnp.zeros_like(right_pick))
    pattern_len = pattern_rows.shape[0]
    left_pick = left_pick.reshape(pattern_len, cap_left, block_size, block_size)
    right_pick = right_pick.reshape(pattern_len, cap_left, block_size, block_size)
    partial_sum = jnp.einsum(
        "pqab,pqbc->pac", left_pick, right_pick, preferred_element_type=jnp.float32
    )
    share = lax.psum_scatter(partial_sum[None, None], "depth", scatter_dimension=2, tiled=True)
    return jnp.log1p(share).astype(jnp.bfloat16)


def solution(mesh):
    in_specs = (
        P(("row", "depth"), "col", None, None, None),
        P(("row", "depth"), "col", None),
        P(("row", "depth"), "col"),
        P("row", "col", None, None),
    )
    out_specs = P("row", "col", "depth", None, None)
    return jax.shard_map(body, mesh=mesh, in_specs=in_specs, out_specs=out_specs, check_vma=False)
```

profile of v0, /device:TPU:4, one launch (start us, length us, event | category | flops | bytes accessed | tf_op | source)
XLA Modules:
  0.0 247.1 jit_solution(16107756363442089522)
XLA Ops:
  8.5 0.7 fusion.30
  9.4 2.1 scatter_fusion.1
  11.5 21.9 %all_to_all.30 = bf16[16,1,2,128,128]{4,3,2,1,0:T(8,128)(2,1)} all-to-all(bf16[16,1,2,128,128]{4,3,2,1,0:T(8,128)(2,1)S(1)} %bitcast.96), channel_id=1, replica_groups=mesh['row'=4,'col'=16,'depth'=8] {'col'}, dimensions={0} | all-to-all | bytes 2097152 | tf_op jit(solution)/shard_map/all_to_all | solution.py:79
  33.6 1.1 scatter_fusion
  34.8 25.3 %all_to_all.31 = bf16[8,1,2,128,128]{4,3,2,1,0:T(8,128)(2,1)} all-to-all(bf16[8,1,2,128,128]{4,3,2,1,0:T(8,128)(2,1)S(1)} %bitcast.97), channel_id=1, replica_groups=mesh['row'=4,'col'=16,'depth'=8] {'depth'}, dimensions={0} | all-to-all | bytes 1048576 | tf_op jit(solution)/shard_map/all_to_all | solution.py:59
  60.1 0.8 scatter_custom_fusion.2
  60.9 0.7 reshape.1075
  61.6 5.9 %all-to-all-start.3 = ((s32[16,1,2]{2,1,0:T(1,128)}), s32[16,1,2]{2,1,0:T(1,128)S(1)}, u32[]{:S(2)}, u32[]{:S(2)}) async-start(s32[16,1,2]{2,1,0:T(1,128)} %bitcast.15), calls=%async_computation.3 | async-start | bytes 16384 | tf_op jit(solution)/shard_map/all_to_all | solution.py:80
  67.5 0.8 scatter_custom_fusion.1
  68.9 2.3 all-to-all-done.3
  71.2 3.3 %all-to-all-start.1 = ((s32[8,1,2]{2,1,0:T(1,128)}), s32[8,1,2]{2,1,0:T(1,128)S(1)}, u32[]{:S(2)}, u32[]{:S(2)}) async-start(s32[8,1,2]{2,1,0:T(1,128)} %bitcast.11), calls=%async_computation.1 | async-start | bytes 8192 | tf_op jit(solution)/shard_map/all_to_all | solution.py:60
  74.6 7.4 %all-to-all-done.1 = s32[8,1,2]{2,1,0:T(1,128)S(1)} async-done(((s32[8,1,2]{2,1,0:T(1,128)}), s32[8,1,2]{2,1,0:T(1,128)S(1)}, u32[]{:S(2)}, u32[]{:S(2)}) %all-to-all-start.1) | async-done | bytes 96 | tf_op jit(solution)/shard_map/all_to_all | solution.py:60
  82.7 6.2 %all-to-all-start.4 = ((s32[4,16,1,2]{1,3,2,0:T(2,128)}), s32[4,16,1,2]{1,3,2,0:T(2,128)S(1)}, u32[]{:S(2)}, u32[]{:S(2)}) async-start(s32[4,16,1,2]{1,3,2,0:T(2,128)} %broadcast_in_dim.130), calls=%async_computation.4 | async-start | bytes 8192 | tf_op jit(solution)/shard_map/all_to_all | solution.py:33
  89.0 7.5 %all-to-all-done.4 = s32[4,16,1,2]{1,3,2,0:T(2,128)S(1)} async-done(((s32[4,16,1,2]{1,3,2,0:T(2,128)}), s32[4,16,1,2]{1,3,2,0:T(2,128)S(1)}, u32[]{:S(2)}, u32[]{:S(2)}) %all-to-all-start.4) | async-done | bytes 544 | tf_op jit(solution)/shard_map/all_to_all | solution.py:33
  97.2 6.9 %all-to-all-start.2 = ((s32[16,8,1,2]{1,3,2,0:T(2,128)}), s32[16,8,1,2]{1,3,2,0:T(2,128)S(1)}, u32[]{:S(2)}, u32[]{:S(2)}) async-start(s32[16,8,1,2]{1,3,2,0:T(2,128)} %broadcast_in_dim.125), calls=%async_computation.2 | async-start | bytes 32768 | tf_op jit(solution)/shard_map/all_to_all | solution.py:33
  104.7 3.6 %all-to-all-done.2 = s32[16,8,1,2]{1,3,2,0:T(2,128)S(1)} async-done(((s32[16,8,1,2]{1,3,2,0:T(2,128)}), s32[16,8,1,2]{1,3,2,0:T(2,128)S(1)}, u32[]{:S(2)}, u32[]{:S(2)}) %all-to-all-start.2) | async-done | bytes 1056 | tf_op jit(solution)/shard_map/all_to_all | solution.py:33
  108.6 0.8 gather_fusion.1
  111.6 12.6 %all-gather.7.cloned.1.call-done = bf16[64,1,2,128,128]{4,3,2,1,0:T(8,128)(2,1)} async-done(((bf16[16,1,2,128,128]{4,3,2,1,0:T(8,128)(2,1)}), bf16[64,1,2,128,128]{4,3,2,1,0:T(8,128)(2,1)}) %all-gather.7.cloned.1.call-update) | async-done | bytes 4194320 | tf_op jit(solution)/shard_map/all_gather | solution.py:83
  124.2 3.1 %gather_fusion.3 = bf16[64,128,128]{2,1,0:T(8,128)(2,1)S(1)} fusion(bf16[128,128,128]{2,1,0:T(8,128)(2,1)} %bitcast.103, s32[1024]{0:T(1024)S(1)} %pad_clamp_fusion), kind=kCustom, calls=%fused_computation.3 | custom fusion | bytes 4194560 | tf_op jit(solution)/shard_map/jit(_take)/gather | solution.py:107
  127.3 55.0 %all-gather.5.cloned.1.call-done = bf16[128,1,2,128,128]{4,3,2,1,0:T(8,128)(2,1)} async-done(((bf16[8,1,2,128,128]{4,3,2,1,0:T(8,128)(2,1)}), bf16[128,1,2,128,128]{4,3,2,1,0:T(8,128)(2,1)}) %all-gather.5.cloned.1.call-update) | async-done | bytes 8388624 | tf_op jit(solution)/shard_map/all_gather | solution.py:63
  182.3 5.6 %gather_fusion = bf16[64,128,128]{2,1,0:T(8,128)(2,1)} fusion(bf16[256,128,128]{2,1,0:T(8,128)(2,1)} %bitcast.104, s32[1024]{0:T(1024)S(1)} %pad_clamp_fusion.3), kind=kCustom, calls=%fused_computation | custom fusion | bytes 4194560 | tf_op jit(solution)/shard_map/jit(_take)/gather | solution.py:95
  187.9 3.7 %fusion.7 = f32[1,1,32,128,128]{4,3,2,1,0:T(8,128)} fusion(bf16[32,2,128,128]{3,2,1,0:T(8,128)(2,1)S(1)} %bitcast.99, pred[32,2]{1,0:T(8,128)(4,1)S(1)} %copy.52, pred[32,2]{1,0:T(8,128)(4,1)S(1)} %get-tuple-element.5, bf16[32,2,128,128]{3,2,1,0:T(8,128)(2,1)} %bitcast.100, pred[32,2]{1,0:T(8,128)(4,1)S(1)} %copy.38), kind=kOutput, calls=%fused_computation.15 | convolution fusion | flops 271581184 | bytes 6291648 | tf_op jit(solution)/shard_map/pqab,pqbc->pac/dot_general | solution.py:112
  191.6 47.2 %reduce-scatter.2.cloned.1.call-done = f32[1,1,4,128,128]{4,3,2,1,0:T(8,128)} async-done(((f32[1,1,32,128,128]{4,3,2,1,0:T(8,128)}), f32[1,1,4,128,128]{4,3,2,1,0:T(8,128)}) %reduce-scatter.2.cloned.1.call-update) | async-done | bytes 262160 | tf_op jit(solution)/shard_map/reduce_scatter | solution.py:115
  238.9 1.7 log-plus-one_convert_fusion
  (60 shorter events, 6.9 us)
Async XLA Ops:
  6.5 117.7 %all-gather.7.cloned.1.call-start = ((), (), s32[]{:S(2)}) async-start(), calls=%async_computation.9 | async-start | bytes 5242880 | tf_op jit(solution)/shard_map/all_gather | solution.py:83
  11.5 22.1 %copy-start = (bf16[1,1,16,128,128]{4,3,2,1,0:T(8,128)(2,1)S(1)}, bf16[1,1,16,128,128]{4,3,2,1,0:T(8,128)(2,1)}, u32[]{:S(2)}) copy-start(bf16[1,1,16,128,128]{4,3,2,1,0:T(8,128)(2,1)} %param.4) | copy-start | bytes 1572868
  33.5 34.0 %copy-start.1 = (s32[1,1,32,2]{2,3,1,0:T(2,128)S(1)}, s32[1,1,32,2]{2,3,1,0:T(2,128)}, u32[]{:S(2)}) copy-start(s32[1,1,32,2]{2,3,1,0:T(2,128)} %param.7) | copy-start | bytes 772
  33.5 148.8 %all-gather.5.cloned.1.call-start = ((), (), s32[]{:S(2)}) async-start(), calls=%async_computation.8 | async-start | bytes 8912896 | tf_op jit(solution)/shard_map/all_gather | solution.py:63
  61.6 9.6 %all-to-all-start.3 = ((s32[16,1,2]{2,1,0:T(1,128)}), s32[16,1,2]{2,1,0:T(1,128)S(1)}, u32[]{:S(2)}, u32[]{:S(2)}) async-start(s32[16,1,2]{2,1,0:T(1,128)} %bitcast.15), calls=%async_computation.3 | async-start | bytes 16384 | tf_op jit(solution)/shard_map/all_to_all | solution.py:80
  71.2 10.9 %all-to-all-start.1 = ((s32[8,1,2]{2,1,0:T(1,128)}), s32[8,1,2]{2,1,0:T(1,128)S(1)}, u32[]{:S(2)}, u32[]{:S(2)}) async-start(s32[8,1,2]{2,1,0:T(1,128)} %bitcast.11), calls=%async_computation.1 | async-start | bytes 8192 | tf_op jit(solution)/shard_map/all_to_all | solution.py:60
  82.7 13.9 %all-to-all-start.4 = ((s32[4,16,1,2]{1,3,2,0:T(2,128)}), s32[4,16,1,2]{1,3,2,0:T(2,128)S(1)}, u32[]{:S(2)}, u32[]{:S(2)}) async-start(s32[4,16,1,2]{1,3,2,0:T(2,128)} %broadcast_in_dim.130), calls=%async_computation.4 | async-start | bytes 8192 | tf_op jit(solution)/shard_map/all_to_all | solution.py:33
  97.2 11.1 %all-to-all-start.2 = ((s32[16,8,1,2]{1,3,2,0:T(2,128)}), s32[16,8,1,2]{1,3,2,0:T(2,128)S(1)}, u32[]{:S(2)}, u32[]{:S(2)}) async-start(s32[16,8,1,2]{1,3,2,0:T(2,128)} %broadcast_in_dim.125), calls=%async_computation.2 | async-start | bytes 32768 | tf_op jit(solution)/shard_map/all_to_all | solution.py:33
  104.1 134.8 %reduce-scatter.2.cloned.1.call-start = ((), (), s32[]{:S(2)}) async-start(), calls=%async_computation.7 | async-start | bytes 2359296 | tf_op jit(solution)/shard_map/reduce_scatter | solution.py:115
Sparse Core Ops, SparseCore 0:
  33.6 90.5 all-gather.6
  126.3 55.9 all-gather.4
  191.8 47.0 reduce-scatter.1
where the time goes:
time: 248 us; the launch traced here: 247 us
  waiting for transfers between devices  136 us (55%)
  blocking collectives  47.3 us (19%)
  starting transfers between devices  22.4 us (9%)
  local copies, waits for them, and re-layouts  20.1 us (8%)
  between operations  14 us (6%)
  other arithmetic  4 us (2%)
  matrix products  3.74 us (2%)
    all_gather x1, waiting for transfers between devices, body(): lax.all_gather(left_vals[None], 'col', axis=0, tiled=True)  55 us
    reduce_scatter x1, waiting for transfers between devices, body(): lax.psum_scatter(partial_sum[None, None], 'depth', scatter_dimension=2, t...  47.2 us
    all_to_all x1, blocking collectives, body(): lax.all_to_all(left_vals, 'depth', split_axis=0, concat_axis=0, tiled=True)  25.3 us
    all_to_all x1, blocking collectives, body(): lax.all_to_all(right_vals, 'col', split_axis=0, concat_axis=0, tiled=True)  21.9 us
    all_to_all x2, starting transfers between devices, gather_by_exchange(): return lax.all_to_all(copies, axis, split_axis=0, concat_axis=0, tiled=True)  13.1 us
    all_gather x1, waiting for transfers between devices, body(): lax.all_gather(right_vals[None], 'row', axis=0, tiled=True)  12.6 us
    all_to_all x2, waiting for transfers between devices, gather_by_exchange(): return lax.all_to_all(copies, axis, split_axis=0, concat_axis=0, tiled=True)  11.2 us
    all_to_all x1, waiting for transfers between devices, body(): lax.all_to_all(left_cols, 'depth', split_axis=0, concat_axis=0, tiled=True)  7.44 us
  transfers between devices with their start and end apart: 7, of which 7 were waited for; matrix products, arithmetic and copies ran while one was open for 5% of the time, Pallas kernels for 0%

commit v1 on v0

--- a/solution.py
+++ b/solution.py
@@ -60,7 +60,9 @@
         lax.all_to_all(left_cols, "depth", split_axis=0, concat_axis=0, tiled=True),
     )
     left_vals, left_cols = (
-        lax.all_gather(left_vals[None], "col", axis=0, tiled=True),
+        jnp.concatenate(
+            lax.all_to_all(jnp.stack([left_vals[None]] * lax.axis_size("col")), "col", 0, 0), axis=0
+        ),
         gather_by_exchange(left_cols, "col", columns),
     )
     left_shape = left_cols.shape

time: 248 us -> 349 us (1.41)
  waiting for transfers between devices: 136 us -> 241 us
  blocking collectives: 47.3 us -> 18.3 us
  starting transfers between devices: 22.4 us -> 40 us
  local copies, waits for them, and re-layouts: 20.1 us -> 27 us
    all_gather x1, waiting for transfers between devices: 12.6 us -> 112 us  [body(): lax.all_gather(right_vals[None], 'row', axis=0, tiled=True)]
    all_to_all x0 -> x2, waiting for transfers between devices: none -> 55.7 us  [the longest x1 39.1 us: body(): lax.all_to_all(jnp.stack([left_vals[None]] * lax.axis_size('col')), 'col'...]
    all_gather x1 -> x0, waiting for transfers between devices: 55 us -> none  [body(): lax.all_gather(left_vals[None], 'col', axis=0, tiled=True)]
    all_to_all x1 -> x0, blocking collectives: 25.3 us -> none  [body(): lax.all_to_all(left_vals, 'depth', split_axis=0, concat_axis=0, tiled=True)]
    all_to_all x0 -> x2, starting transfers between devices: none -> 12 us  [the longest x1 8.47 us: body(): lax.all_to_all(jnp.stack([left_vals[None]] * lax.axis_size('col')), 'col'...]
    reduce_scatter x1, waiting for transfers between devices: 47.2 us -> 55 us  [body(): lax.psum_scatter(partial_sum[None, None], 'depth', scatter_dimension=2, t...]
    another operation x0 -> x1, local copies, waits for them, and re-layouts: none -> 5.33 us  [body(): jnp.stack([left_vals[None]] * lax.axis_size('col'))]
    all_to_all x1, starting transfers between devices: 3.28 us -> 6.93 us  [body(): lax.all_to_all(left_cols, 'depth', split_axis=0, concat_axis=0, tiled=True)]
  transfers between devices with their start and end apart: 7 -> 8, of which waited for: 7 -> 8; matrix products, arithmetic and copies ran while one was open for 5% -> 4% of each run, Pallas kernels for 0% -> 0%
where the time goes in v1:
time: 349 us
  waiting for transfers between devices  241 us (69%)
  starting transfers between devices  40 us (11%)
  local copies, waits for them, and re-layouts  27 us (8%)
  blocking collectives  18.3 us (5%)
  between operations  14.3 us (4%)
  other arithmetic  4 us (1%)
  matrix products  3.76 us (1%)
    all_gather x1, waiting for transfers between devices, body(): lax.all_gather(right_vals[None], 'row', axis=0, tiled=True)  112 us
    reduce_scatter x1, waiting for transfers between devices, body(): lax.psum_scatter(partial_sum[None, None], 'depth', scatter_dimension=2, t...  55 us
    all_to_all x1, waiting for transfers between devices, body(): lax.all_to_all(jnp.stack([left_vals[None]] * lax.axis_size('col')), 'col'...  39.1 us
    all_to_all x1, blocking collectives, body(): lax.all_to_all(right_vals, 'col', split_axis=0, concat_axis=0, tiled=True)  18.3 us
    all_to_all x1, waiting for transfers between devices, body(): lax.all_to_all(left_vals, 'depth', split_axis=0, concat_axis=0, tiled=True)  16.6 us
    all_to_all x2, starting transfers between devices, gather_by_exchange(): return lax.all_to_all(copies, axis, split_axis=0, concat_axis=0, tiled=True)  11.9 us
    all_to_all x1, starting transfers between devices, body(): lax.all_to_all(right_cols, 'col', split_axis=0, concat_axis=0, tiled=True)  9.16 us
    all_to_all x1, starting transfers between devices, body(): lax.all_to_all(jnp.stack([left_vals[None]] * lax.axis_size('col')), 'col'...  8.47 us
  transfers between devices with their start and end apart: 8, of which 8 were waited for; matrix products, arithmetic and copies ran while one was open for 4% of the time, Pallas kernels for 0%

profile of v1, /device:TPU:4, one launch (start us, length us, event | category | flops | bytes accessed | tf_op | source)
XLA Modules:
  0.0 348.5 jit_solution(2259339694360486009)
XLA Ops:
  9.2 0.8 scatter_custom_fusion.2
  10.6 9.2 %all-to-all-start.4 = ((s32[16,1,2]{2,1,0:T(1,128)}), s32[16,1,2]{2,1,0:T(1,128)S(1)}, u32[]{:S(2)}, u32[]{:S(2)}) async-start(s32[16,1,2]{2,1,0:T(1,128)} %bitcast.16), calls=%async_computation.4 | async-start | bytes 16384 | tf_op jit(solution)/shard_map/all_to_all | solution.py:82
  21.2 2.4 all-to-all-done.4
  23.5 6.9 %all-to-all-start.2 = ((s32[8,1,2]{2,1,0:T(1,128)}), s32[8,1,2]{2,1,0:T(1,128)S(1)}, u32[]{:S(2)}, u32[]{:S(2)}) async-start(s32[8,1,2]{2,1,0:T(1,128)} %bitcast.12), calls=%async_computation.2 | async-start | bytes 8192 | tf_op jit(solution)/shard_map/all_to_all | solution.py:60
  30.6 7.6 %all-to-all-done.2 = s32[8,1,2]{2,1,0:T(1,128)S(1)} async-done(((s32[8,1,2]{2,1,0:T(1,128)}), s32[8,1,2]{2,1,0:T(1,128)S(1)}, u32[]{:S(2)}, u32[]{:S(2)}) %all-to-all-start.2) | async-done | bytes 96 | tf_op jit(solution)/shard_map/all_to_all | solution.py:60
  38.7 6.2 %all-to-all-start.5 = ((s32[4,16,1,2]{1,3,2,0:T(2,128)}), s32[4,16,1,2]{1,3,2,0:T(2,128)S(1)}, u32[]{:S(2)}, u32[]{:S(2)}) async-start(s32[4,16,1,2]{1,3,2,0:T(2,128)} %broadcast_in_dim.126), calls=%async_computation.5 | async-start | bytes 8192 | tf_op jit(solution)/shard_map/all_to_all | solution.py:33
  45.0 7.6 %all-to-all-done.5 = s32[4,16,1,2]{1,3,2,0:T(2,128)S(1)} async-done(((s32[4,16,1,2]{1,3,2,0:T(2,128)}), s32[4,16,1,2]{1,3,2,0:T(2,128)S(1)}, u32[]{:S(2)}, u32[]{:S(2)}) %all-to-all-start.5) | async-done | bytes 544 | tf_op jit(solution)/shard_map/all_to_all | solution.py:33
  53.2 5.7 %all-to-all-start.3 = ((s32[16,8,1,2]{1,3,2,0:T(2,128)}), s32[16,8,1,2]{1,3,2,0:T(2,128)S(1)}, u32[]{:S(2)}, u32[]{:S(2)}) async-start(s32[16,8,1,2]{1,3,2,0:T(2,128)} %broadcast_in_dim.121), calls=%async_computation.3 | async-start | bytes 32768 | tf_op jit(solution)/shard_map/all_to_all | solution.py:33
  58.9 0.9 broadcast_in_dim.117
  59.8 2.9 scatter_fusion
  62.8 3.5 %all-to-all-start = ((bf16[8,1,2,128,128]{4,3,2,1,0:T(8,128)(2,1)}), bf16[8,1,2,128,128]{4,3,2,1,0:T(8,128)(2,1)S(1)}, u32[]{:S(2)}, u32[]{:S(2)}) async-start(bf16[8,1,2,128,128]{4,3,2,1,0:T(8,128)(2,1)} %bitcast.7), calls=%async_computation | async-start | bytes 1048576 | tf_op jit(solution)/shard_map/all_to_all | solution.py:59
  66.5 1.1 scatter_fusion.1
  67.7 16.6 %all-to-all-done = bf16[8,1,2,128,128]{4,3,2,1,0:T(8,128)(2,1)S(1)} async-done(((bf16[8,1,2,128,128]{4,3,2,1,0:T(8,128)(2,1)}), bf16[8,1,2,128,128]{4,3,2,1,0:T(8,128)(2,1)S(1)}, u32[]{:S(2)}, u32[]{:S(2)}) %all-to-all-start) | async-done | bytes 524320 | tf_op jit(solution)/shard_map/all_to_all | solution.py:59
  84.3 18.3 %all_to_all.38 = bf16[16,1,2,128,128]{4,3,2,1,0:T(8,128)(2,1)} all-to-all(bf16[16,1,2,128,128]{4,3,2,1,0:T(8,128)(2,1)S(1)} %bitcast.93), channel_id=1, replica_groups=mesh['row'=4,'col'=16,'depth'=8] {'col'}, dimensions={0} | all-to-all | bytes 2097152 | tf_op jit(solution)/shard_map/all_to_all | solution.py:81
  102.6 5.3 %stack.3 = bf16[16,1,8,1,2,128,128]{6,5,4,3,2,1,0:T(8,128)(2,1)} broadcast(bf16[8,2,128,128]{3,2,1,0:T(8,128)(2,1)S(1)} %bitcast.95), dimensions={2,4,5,6} | broadcast | bytes 8912896 | tf_op jit(solution)/shard_map/stack | solution.py:64
  108.0 8.5 %all-to-all-start.1 = ((bf16[16,1,8,1,2,128,128]{6,5,4,3,2,1,0:T(8,128)(2,1)}), bf16[16,1,8,1,2,128,128]{6,5,4,3,2,1,0:T(8,128)(2,1)}, u32[]{:S(2)}, u32[]{:S(2)}) async-start(bf16[16,1,8,1,2,128,128]{6,5,4,3,2,1,0:T(8,128)(2,1)} %stack.3), calls=%async_computation.1 | async-start | bytes 16777216 | tf_op jit(solution)/shard_map/all_to_all | solution.py:64
  118.3 0.8 gather_fusion.1
  121.3 112.1 %all-gather.3.cloned.1.call-done = bf16[64,1,2,128,128]{4,3,2,1,0:T(8,128)(2,1)} async-done(((bf16[16,1,2,128,128]{4,3,2,1,0:T(8,128)(2,1)}), bf16[64,1,2,128,128]{4,3,2,1,0:T(8,128)(2,1)}) %all-gather.3.cloned.1.call-update) | async-done | bytes 4194320 | tf_op jit(solution)/shard_map/all_gather | solution.py:85
  233.4 3.1 gather_fusion.3
  236.6 39.1 %all-to-all-done.1 = bf16[16,1,8,1,2,128,128]{6,5,4,3,2,1,0:T(8,128)(2,1)} async-done(((bf16[16,1,8,1,2,128,128]{6,5,4,3,2,1,0:T(8,128)(2,1)}), bf16[16,1,8,1,2,128,128]{6,5,4,3,2,1,0:T(8,128)(2,1)}, u32[]{:S(2)}, u32[]{:S(2)}) %all-to-all-start.1) | async-done | bytes 8388640 | tf_op jit(solution)/shard_map/all_to_all | solution.py:64
  275.6 5.6 %gather_fusion = bf16[64,128,128]{2,1,0:T(8,128)(2,1)} fusion(bf16[256,128,128]{2,1,0:T(8,128)(2,1)} %bitcast.9, s32[1024]{0:T(1024)S(1)} %pad_clamp_fusion.3), kind=kCustom, calls=%fused_computation | custom fusion | bytes 4194560 | tf_op jit(solution)/shard_map/jit(_take)/gather | solution.py:97
  281.2 3.8 %fusion.7 = f32[1,1,32,128,128]{4,3,2,1,0:T(8,128)} fusion(bf16[32,2,128,128]{3,2,1,0:T(8,128)(2,1)S(1)} %bitcast.96, pred[32,2]{1,0:T(8,128)(4,1)S(1)} %copy.52, pred[32,2]{1,0:T(8,128)(4,1)S(1)} %get-tuple-element.5, bf16[32,2,128,128]{3,2,1,0:T(8,128)(2,1)} %bitcast.97, pred[32,2]{1,0:T(8,128)(4,1)S(1)} %copy.38), kind=kOutput, calls=%fused_computation.15 | convolution fusion | flops 271581184 | bytes 6291648 | tf_op jit(solution)/shard_map/pqab,pqbc->pac/dot_general | solution.py:114
  285.0 55.0 %reduce-scatter.2.cloned.1.call-done = f32[1,1,4,128,128]{4,3,2,1,0:T(8,128)} async-done(((f32[1,1,32,128,128]{4,3,2,1,0:T(8,128)}), f32[1,1,4,128,128]{4,3,2,1,0:T(8,128)}) %reduce-scatter.2.cloned.1.call-update) | async-done | bytes 262160 | tf_op jit(solution)/shard_map/reduce_scatter | solution.py:117
  340.0 1.7 log-plus-one_convert_fusion
  (61 shorter events, 9.7 us)
Async XLA Ops:
  10.6 12.9 %all-to-all-start.4 = ((s32[16,1,2]{2,1,0:T(1,128)}), s32[16,1,2]{2,1,0:T(1,128)S(1)}, u32[]{:S(2)}, u32[]{:S(2)}) async-start(s32[16,1,2]{2,1,0:T(1,128)} %bitcast.16), calls=%async_computation.4 | async-start | bytes 16384 | tf_op jit(solution)/shard_map/all_to_all | solution.py:82
  23.5 14.6 %all-to-all-start.2 = ((s32[8,1,2]{2,1,0:T(1,128)}), s32[8,1,2]{2,1,0:T(1,128)S(1)}, u32[]{:S(2)}, u32[]{:S(2)}) async-start(s32[8,1,2]{2,1,0:T(1,128)} %bitcast.12), calls=%async_computation.2 | async-start | bytes 8192 | tf_op jit(solution)/shard_map/all_to_all | solution.py:60
  38.7 13.9 %all-to-all-start.5 = ((s32[4,16,1,2]{1,3,2,0:T(2,128)}), s32[4,16,1,2]{1,3,2,0:T(2,128)S(1)}, u32[]{:S(2)}, u32[]{:S(2)}) async-start(s32[4,16,1,2]{1,3,2,0:T(2,128)} %broadcast_in_dim.126), calls=%async_computation.5 | async-start | bytes 8192 | tf_op jit(solution)/shard_map/all_to_all | solution.py:33
  53.2 9.6 %all-to-all-start.3 = ((s32[16,8,1,2]{1,3,2,0:T(2,128)}), s32[16,8,1,2]{1,3,2,0:T(2,128)S(1)}, u32[]{:S(2)}, u32[]{:S(2)}) async-start(s32[16,8,1,2]{1,3,2,0:T(2,128)} %broadcast_in_dim.121), calls=%async_computation.3 | async-start | bytes 32768 | tf_op jit(solution)/shard_map/all_to_all | solution.py:33
  58.9 7.6 %copy-start = (bf16[1,1,16,128,128]{4,3,2,1,0:T(8,128)(2,1)S(1)}, bf16[1,1,16,128,128]{4,3,2,1,0:T(8,128)(2,1)}, u32[]{:S(2)}) copy-start(bf16[1,1,16,128,128]{4,3,2,1,0:T(8,128)(2,1)} %param.4) | copy-start | bytes 1572868
  62.8 21.5 %all-to-all-start = ((bf16[8,1,2,128,128]{4,3,2,1,0:T(8,128)(2,1)}), bf16[8,1,2,128,128]{4,3,2,1,0:T(8,128)(2,1)S(1)}, u32[]{:S(2)}, u32[]{:S(2)}) async-start(bf16[8,1,2,128,128]{4,3,2,1,0:T(8,128)(2,1)} %bitcast.7), calls=%async_computation | async-start | bytes 1048576 | tf_op jit(solution)/shard_map/all_to_all | solution.py:59
  108.0 9.3 %copy-start.1 = (s32[1,1,32,2]{2,3,1,0:T(2,128)S(1)}, s32[1,1,32,2]{2,3,1,0:T(2,128)}, u32[]{:S(2)}) copy-start(s32[1,1,32,2]{2,3,1,0:T(2,128)} %param.7) | copy-start | bytes 772
  108.0 167.6 %all-to-all-start.1 = ((bf16[16,1,8,1,2,128,128]{6,5,4,3,2,1,0:T(8,128)(2,1)}), bf16[16,1,8,1,2,128,128]{6,5,4,3,2,1,0:T(8,128)(2,1)}, u32[]{:S(2)}, u32[]{:S(2)}) async-start(bf16[16,1,8,1,2,128,128]{6,5,4,3,2,1,0:T(8,128)(2,1)} %stack.3), calls=%async_computation.1 | async-start | bytes 16777216 | tf_op jit(solution)/shard_map/all_to_all | solution.py:64
  116.5 117.0 %all-gather.3.cloned.1.call-start = ((), (), s32[]{:S(2)}) async-start(), calls=%async_computation.9 | async-start | bytes 5242880 | tf_op jit(solution)/shard_map/all_gather | solution.py:85
  117.2 222.8 %reduce-scatter.2.cloned.1.call-start = ((), (), s32[]{:S(2)}) async-start(), calls=%async_computation.8 | async-start | bytes 2359296 | tf_op jit(solution)/shard_map/reduce_scatter | solution.py:117
Sparse Core Ops, SparseCore 0:
  119.4 113.9 all-gather.2
  285.1 54.8 reduce-scatter.1
